TPU v7x, 32 devices: a whole 2x2x4 slice. The times are simulated.
32 devices in a mesh: req: 16 (over z, x, core), kv: 2 (over y).
Axes of the slice: x: 2, y: 2, z: 4, core: 2. Of those that a mesh axis runs over, the one named last changes fastest.
Arguments:
- hidden: bfloat16 [32, 256, 1024], P('req', 'kv'), may hold values from -6 to 6
- queries: bfloat16 [32, 256, 1024], P('req', 'kv'), may hold values from -24 to 24
- span_kv: bfloat16 [32, 256, 8, 128], P('req', 'kv'), may hold values from -48 to 48
- cache: bfloat16 [32, 2048, 8, 128], P('req', 'kv'), may hold values from -48 to 48
- req_order: int32 [32], replicated, may hold values from 0 to 31, each once
- cached_len: int32 [32], replicated, may hold values from 8 to 2048, as said below
- out_weight: bfloat16 [1024, 1024], replicated, may hold values from -0.1875 to 0.1875
- norm_gain: float32 [1024], replicated, may hold values from 0.1 to 1.9
- expert_ids: int32 [8192, 8], P(('req', 'kv')), may hold values from 0 to 15, all different within a row; in each aligned block of 256 rows (0 to 255, 256 to 511, ...) at most 256 rows name the same one
- expert_weights: float32 [8192, 8], P(('req', 'kv')), may hold values from 0.05 to 0.5
- w_experts: bfloat16 [16, 3, 1024, 512], P('req', None, None, 'kv'), may hold values from -0.25 to 0.25
- block_map: int32 [32, 128], P('req'), may hold values from 0 to 4095, as said below
Outputs:
- layer_out: bfloat16 [32, 256, 1024], P('req', 'kv')
- decode_pool: bfloat16 [4096, 8, 16, 128], P('req', 'kv')
Inputs may be any that keep to these rules, and one draw needn't show every extreme that they name: `cached_len`: some request fills its cache. `block_map`: a permutation of the 4096 pool pages; pool page s belongs to req index s // 256; the pages that one kv index holds of the slots of one req index (positions of its cache share) go to every req index equally often. `expert_ids`: in the rows of one device no expert is named more than 256 times.
All inputs are finite; a program needn't handle non-finite values.
Results may differ from a plain program's by a relative error of at most 0.023.
Values may be sent and summed in bfloat16 or wider, within the bound.
No kernel may reach another device: no remote copies, remote signals or barrier semaphores. Data moves between devices by JAX's collectives and lax.ppermute only.
A program may use at most 128 MiB of HBM per device.

v0:
```python
import math
import jax
import jax.numpy as jnp
from jax import lax
from jax.sharding import PartitionSpec as P

BLOCK = 16


def lookup_lengths(req_order, cached_len, count):
    start = lax.axis_index("req") * count
    mine = lax.dynamic_slice_in_dim(req_order, start, count)
    match = mine[:, None] == jnp.arange(cached_len.shape[0], dtype=jnp.int32)[None, :]
    return jnp.sum(jnp.where(match, cached_len[None, :], 0), axis=1)


def score_block(query_rows, cache_rows, span_rows):
    span_count, group_count, width = query_rows.shape
    head_dim = cache_rows.shape[-1] // 2
    per_group = width // head_dim
    query_split = query_rows.reshape(span_count, group_count, per_group, head_dim)
    key_rows = jnp.concatenate([cache_rows[..., :head_dim], span_rows[..., :head_dim]], axis=0)
    value_rows = jnp.concatenate([cache_rows[..., head_dim:], span_rows[..., head_dim:]], axis=0)
    scores = jnp.einsum(
        "igsd,pgd->gsip", query_split, key_rows, preferred_element_type=jnp.float32
    ) * (1.0 / math.sqrt(head_dim))
    return (scores, value_rows)


def soft_weights(scores, allowed, value_rows):
    masked = jnp.where(allowed, scores, -1e30)
    row_max = jnp.max(masked, axis=-1, keepdims=True)
    probability = jnp.where(allowed, jnp.exp(masked - row_max), 0.0)
    prob_sum = jnp.sum(probability, axis=-1)
    weighted = jnp.einsum(
        "gsip,pgd->igsd",
        probability.astype(jnp.bfloat16),
        value_rows,
        preferred_element_type=jnp.float32,
    )
    return (weighted, jnp.transpose(row_max[..., 0], (2, 0, 1)), jnp.transpose(prob_sum, (2, 0, 1)))


def whole_request(operands):
    query_rows, cache_rows, span_rows, length = operands
    scores, value_rows = score_block(query_rows, cache_rows, span_rows)
    cached = cache_rows.shape[0]
    position = jnp.arange(scores.shape[-1])[None, :]
    query_pos = jnp.arange(query_rows.shape[0])[:, None]
    allowed = jnp.where(position < cached, position < length, position - cached <= query_pos)
    weighted, row_max, prob_sum = soft_weights(scores, allowed, value_rows)
    result = weighted / prob_sum[..., None]
    return result.reshape(query_rows.shape).astype(jnp.bfloat16)


def place_pages(page_rows, slot_numbers, slots_dev):
    owner_index = slot_numbers // slots_dev
    arrangement = jnp.argsort(owner_index, stable=True)
    return (page_rows[arrangement], (slot_numbers % slots_dev)[arrangement])


def body(
    hidden,
    queries,
    span_kv,
    cache,
    req_order,
    cached_len,
    out_weight,
    norm_gain,
    expert_ids,
    expert_weights,
    w_experts,
    block_map,
):
    local_reqs, local_tokens, width_model = hidden.shape
    row_count = local_reqs * local_tokens
    req_count = lax.axis_size("req")
    kv_count = lax.axis_size("kv")
    kv_heads = span_kv.shape[2]
    head_pair = span_kv.shape[3]
    group_width = queries.shape[2] // kv_heads
    group_count = kv_heads // kv_count
    slots_dev = local_reqs * block_map.shape[1]
    lengths = lookup_lengths(req_order, cached_len, local_reqs)
    queries_grouped = queries.reshape(local_reqs, local_tokens, kv_heads, group_width)
    cache_heads, span_heads, query_heads = (
        lax.all_to_all(cache, "kv", split_axis=2, concat_axis=1, tiled=True),
        lax.all_to_all(span_kv, "kv", split_axis=2, concat_axis=1, tiled=True),
        lax.all_to_all(queries_grouped, "kv", split_axis=2, concat_axis=1, tiled=True),
    )
    attn_heads = lax.map(whole_request, (query_heads, cache_heads, span_heads, lengths))
    attn = lax.all_to_all(attn_heads, "kv", split_axis=1, concat_axis=2, tiled=True).reshape(
        row_count, kv_heads * group_width
    )
    page_total = block_map.shape[1]
    visible = jnp.arange(cache_heads.shape[1])[None, :] < lengths[:, None]
    visible_cache = jnp.where(visible[:, :, None, None], cache_heads, jnp.zeros((), jnp.bfloat16))
    page_rows = (
        visible_cache.reshape(local_reqs, page_total, BLOCK, group_count, head_pair)
        .transpose(0, 1, 3, 2, 4)
        .reshape(local_reqs * page_total, group_count, BLOCK, head_pair)
    )
    sorted_pages, local_slot = place_pages(page_rows, block_map.reshape(-1), slots_dev)
    per_owner = sorted_pages.shape[0] // req_count
    outgoing = sorted_pages.reshape(req_count, per_owner, group_count, BLOCK, head_pair)
    arrived, where_to = (
        lax.all_to_all(outgoing, "req", split_axis=0, concat_axis=0, tiled=True),
        lax.all_to_all(
            local_slot.reshape(req_count, per_owner), "req", split_axis=0, concat_axis=0, tiled=True
        ),
    )
    decode_pool = (
        jnp.zeros((slots_dev, group_count, BLOCK, head_pair), jnp.bfloat16)
        .at[where_to.reshape(-1)]
        .set(arrived.reshape(-1, group_count, BLOCK, head_pair))
    )
    residual = hidden.reshape(row_count, width_model).astype(jnp.float32) + jnp.dot(
        attn, out_weight, preferred_element_type=jnp.float32
    )
    inverse_rms = lax.rsqrt(jnp.mean(residual * residual, axis=-1, keepdims=True) + 1e-05)
    normed = (residual * inverse_rms * norm_gain).astype(jnp.bfloat16)
    top_count = expert_ids.shape[1]
    exp_dev = w_experts.shape[0]
    experts = exp_dev * req_count
    capacity = min(row_count, 2 * row_count * top_count // experts)
    chosen = expert_ids.reshape(-1)
    onehot = (chosen[:, None] == jnp.arange(experts, dtype=jnp.int32)[None, :]).astype(jnp.int32)
    slot_rank = jnp.sum(onehot * (jnp.cumsum(onehot, axis=0) - 1), axis=1)
    target = chosen * capacity + slot_rank
    source_row = jnp.arange(chosen.shape[0]) // top_count
    buffer = (
        jnp.zeros((experts * capacity, width_model), jnp.bfloat16)
        .at[target]
        .set(normed[source_row])
        .reshape(experts, capacity, width_model)
    )
    full_weights = lax.all_gather(w_experts, "kv", axis=3, tiled=True)
    slot_block = lax.all_to_all(buffer, "req", split_axis=0, concat_axis=0, tiled=True)
    source_count = slot_block.shape[0] // exp_dev
    grouped = slot_block.reshape(source_count, exp_dev, slot_block.shape[1], width_model)
    gate_act = jnp.einsum(
        "sejd,edf->sejf", grouped, full_weights[:, 0], preferred_element_type=jnp.float32
    )
    up_act = jnp.einsum(
        "sejd,edf->sejf", grouped, full_weights[:, 1], preferred_element_type=jnp.float32
    )
    activated = (jax.nn.silu(gate_act) * up_act).astype(jnp.bfloat16)
    expert_out = jnp.einsum(
        "sejf,edf->sejd", activated, full_weights[:, 2], preferred_element_type=jnp.float32
    ).astype(jnp.bfloat16)
    returned = lax.all_to_all(
        expert_out.reshape(slot_block.shape), "req", split_axis=0, concat_axis=0, tiled=True
    )
    picked = returned.reshape(experts * capacity, width_model)[target].reshape(
        row_count, top_count, width_model
    )
    expert_sum = jnp.sum(expert_weights[..., None] * picked.astype(jnp.float32), axis=1)
    layer_out = (
        (residual + expert_sum).astype(jnp.bfloat16).reshape(local_reqs, local_tokens, width_model)
    )
    return (layer_out, decode_pool)


def solution(mesh):
    return jax.shard_map(
        body,
        mesh=mesh,
        in_specs=(
            P("req", "kv", None),
            P("req", "kv", None),
            P("req", "kv", None, None),
            P("req", "kv", None, None),
            P(),
            P(),
            P(),
            P(),
            P(("req", "kv"), None),
            P(("req", "kv"), None),
            P("req", None, None, "kv"),
            P("req", None),
        ),
        out_specs=(P("req", "kv", None), P("req", "kv", None, None)),
        check_vma=False,
    )
```

profile of v0, /device:TPU:11, one launch (start us, length us, event | category | flops | bytes accessed | tf_op | source)
XLA Modules:
  0.0 748.4 jit_solution(12969157909613193286)
XLA Ops:
  7.2 2.1 copy.81
  9.3 3.5 all-to-all-start.1
  12.8 1.3 copy.83
  14.1 0.8 copy.84
  14.9 5.2 all-to-all-done.1
  20.1 3.5 all-to-all-start.2
  24.0 5.0 copy.78
  29.0 1.0 all-to-all-done.2
  30.1 5.6 all-to-all-start
  35.7 4.5 reduce-window.6
  41.8 3.2 sort.17
  47.7 1.1 copy.82
  48.8 2.2 all_to_all.74
  51.0 1.0 copy.86
  52.0 28.7 %all-to-all-done = bf16[2,1024,8,128]{3,1,0,2:T(8,128)(2,1)} async-done(((bf16[2,1024,8,128]{3,1,0,2:T(8,128)(2,1)}), bf16[2,1024,8,128]{3,1,0,2:T(8,128)(2,1)}, u32[]{:S(2)}, u32[]{:S(2)}) %all-to-all-start) | async-done | bytes 4194336 | tf_op jit(solution)/shard_map/all_to_all | solution.py:88
  80.7 4.6 copy.80
  85.3 104.1 %while.12 = (s32[]{:T(128)}, bf16[2,256,4,128]{3,2,0,1:T(4,128)(2,1)}, bf16[2,2048,4,128]{3,1,2,0:T(8,128)(2,1)}, bf16[2,256,4,128]{1,3,2,0:T(8,128)(2,1)}, s32[...) while((s32[]{:T(128)}, bf16[2,256,4,128]{3,2,0,1:T(4,128)(2,1)}, ...), condition=%wide.region_4.5_spmd, body=%wide.region_1.4_spmd.sunk | while | flops 1251877888 | bytes 80653984 | solution.py:92
  85.3 3.0 constant_dynamic-slice_fusion.5
  88.3 4.0 copy.115
  92.3 2.8 fusion.64
  95.8 0.7 constant_dynamic-slice_fusion.4
  96.5 1.1 copy.114
  97.6 9.2 %fusion.65 = f32[4,2304,256,2]{2,1,3,0:T(8,128)} fusion(bf16[256,4,2,64]{0,3,2,1:T(8,128)(2,1)S(1)} %bitcast.190, bf16[256,4,64]{0,2,1:T(8,128)(2,1)} %get-tuple-element.183, bf16[2048,4,64]{0,2,1:T(8,128)(2,1)} %get-tuple-element.184), kind=kOutput, calls=%fused_computation.24.clone.1 | convolution fusion | flops 606339072 | bytes 20316160 | tf_op jit(solution)/shard_map/while/body/eval_jaxpr/igsd,pgd->gsip/dot_general | solution.py:24
  106.9 1.2 dynamic_slice.41
  108.7 2.7 fusion.66
  111.4 19.4 %fusion.67 = (f32[4,2,256]{2,1,0:T(2,128)S(1)}, bf16[4,2,256,2304]{2,3,1,0:T(8,128)(2,1)}) fusion(f32[4,2304,256,2]{2,1,3,0:T(8,128)} %fusion.65, pred[256,2304]{0,1:T(8,128)(4,1)} %fusion.66), kind=kOutput, calls=%fused_computation.99.clone.1 | output fusion | flops 37751040 | bytes 28909568 | tf_op jit(solution)/shard_map/while/body/eval_jaxpr/sub | solution.py:33
  130.9 5.5 fusion.68
  136.5 0.8 constant_dynamic-update-slice_fusion.2
  137.3 3.0 constant_dynamic-slice_fusion.5
  140.4 4.0 copy.115
  144.4 2.8 fusion.64
  147.9 0.7 constant_dynamic-slice_fusion.4
  148.6 1.1 copy.114
  149.7 9.2 %fusion.65 = f32[4,2304,256,2]{2,1,3,0:T(8,128)} fusion(bf16[256,4,2,64]{0,3,2,1:T(8,128)(2,1)S(1)} %bitcast.190, bf16[256,4,64]{0,2,1:T(8,128)(2,1)} %get-tuple-element.183, bf16[2048,4,64]{0,2,1:T(8,128)(2,1)} %get-tuple-element.184), kind=kOutput, calls=%fused_computation.24.clone.1 | convolution fusion | flops 606339072 | bytes 20316160 | tf_op jit(solution)/shard_map/while/body/eval_jaxpr/igsd,pgd->gsip/dot_general | solution.py:24
  158.9 1.2 dynamic_slice.41
  160.8 2.7 fusion.66
  163.5 19.4 %fusion.67 = (f32[4,2,256]{2,1,0:T(2,128)S(1)}, bf16[4,2,256,2304]{2,3,1,0:T(8,128)(2,1)}) fusion(f32[4,2304,256,2]{2,1,3,0:T(8,128)} %fusion.65, pred[256,2304]{0,1:T(8,128)(4,1)} %fusion.66), kind=kOutput, calls=%fused_computation.99.clone.1 | output fusion | flops 37751040 | bytes 28909568 | tf_op jit(solution)/shard_map/while/body/eval_jaxpr/sub | solution.py:33
  182.9 5.5 fusion.68
  188.6 0.8 constant_dynamic-update-slice_fusion.2
  189.4 3.6 all-to-all-start.3
  193.1 1.9 gather_fusion.1
  196.4 2.0 all-to-all-done.3
  198.4 10.7 %all-to-all-start.6 = ((s32[16,1,16]{2,1,0:T(1,128)}), s32[16,1,16]{2,1,0:T(1,128)S(1)}, u32[]{:S(2)}, u32[]{:S(2)}) async-start(s32[16,1,16]{2,1,0:T(1,128)} %all_to_all.84), calls=%async_computation.6 | async-start | bytes 16384 | tf_op jit(solution)/shard_map/all_to_all | solution.py:109
  209.3 1.2 reshape.267
  210.5 2.0 multiply_reduce_fusion
  212.5 0.9 multiply_convert_fusion
  213.5 33.0 %scatter_custom_fusion = bf16[4096,1024]{1,0:T(8,128)(2,1)} fusion(s32[2048]{0:T(1024)S(1)} %bitcast.205, bf16[256,1024]{1,0:T(8,128)(2,1)} %multiply_convert_fusion, s32[2048]{0:T(1024)S(1)} %broadcast_clamp_fusion.1, bf16[]{:T(256)} %constant.114.clone.1), kind=kCustom, calls=%fused_computation.49 | custom fusion | bytes 8389120 | tf_op jit(solution)/shard_map/scatter | solution.py:135
  246.4 6.4 all-to-all-start.4
  253.5 2.6 select_bitcast_fusion
  256.1 3.3 copy.96
  259.4 5.2 gather_fusion.2
  264.6 170.4 %all-to-all-done.4 = bf16[16,256,1024]{2,1,0:T(8,128)(2,1)} async-done(((bf16[16,256,1024]{2,1,0:T(8,128)(2,1)}), bf16[16,256,1024]{2,1,0:T(8,128)(2,1)}, u32[]{:S(2)}, u32[]{:S(2)}) %all-to-all-start.4) | async-done | bytes 8388640 | tf_op jit(solution)/shard_map/all_to_all | solution.py:139
  435.0 4.9 all-to-all-start.7
  440.6 46.2 %all-gather.2.cloned.1.call-done = bf16[1,3,1024,512]{3,2,1,0:T(8,128)(2,1)} async-done(((bf16[1,3,1024,256]{3,2,1,0:T(8,128)(2,1)}), bf16[1,3,1024,512]{3,2,1,0:T(8,128)(2,1)}) %all-gather.2.cloned.1.call-update) | async-done | bytes 3145744 | tf_op jit(solution)/shard_map/all_gather | solution.py:138
  486.8 11.4 %fusion.38 = f32[16,256,512]{2,1,0:T(8,128)} fusion(bf16[16,256,1024]{2,1,0:T(8,128)(2,1)} %all-to-all-done.4, bf16[1,3,1024,512]{3,2,1,0:T(8,128)(2,1)} %all-gather.2.cloned.1.call-done), kind=kOutput, calls=%fused_computation.58 | convolution fusion | flops 4294967296 | bytes 17825792 | tf_op jit(solution)/shard_map/sejd,edf->sejf/dot_general | solution.py:142
  498.2 16.0 %convolution_convert_fusion = bf16[16,256,1024]{2,1,0:T(8,128)(2,1)} fusion(f32[16,256,512]{2,1,0:T(8,128)} %fusion.38, bf16[16,256,1024]{2,1,0:T(8,128)(2,1)} %all-to-all-done.4, bf16[1,3,1024,512]{3,2,1,0:T(8,128)(2,1)} %all-gather.2.cloned.1.call-done), kind=kOutput, calls=%fused_computation.47 | convolution fusion | flops 8606711808 | bytes 27262976 | tf_op jit(solution)/shard_map/sejf,edf->sejd/dot_general | solution.py:149
  514.2 18.2 %all-to-all-done.7 = bf16[16,16,4,16,128]{4,3,2,1,0:T(8,128)(2,1)} async-done(((bf16[16,16,4,16,128]{4,3,2,1,0:T(8,128)(2,1)}), bf16[16,16,4,16,128]{4,3,2,1,0:T(8,128)(2,1)}, u32[]{:S(2)}, u32[]{:S(2)}) %all-to-all-start.7) | async-done | bytes 4194336 | tf_op jit(solution)/shard_map/all_to_all | solution.py:108
  532.4 5.3 all-to-all-start.5
  539.1 3.1 broadcast_in_dim.106
  542.2 33.5 %scatter_fusion = bf16[256,4,16,128]{3,2,1,0:T(8,128)(2,1)} fusion(bf16[256,4,16,128]{3,2,1,0:T(8,128)(2,1)} %broadcast_in_dim.106, s32[256]{0:T(256)S(1)} %bitcast.209, bf16[256,4,16,128]{3,2,1,0:T(8,128)(2,1)} %bitcast.57), kind=kCustom, calls=%fused_computation.5 | custom fusion | bytes 12583936 | tf_op jit(solution)/shard_map/scatter | solution.py:116
  575.7 144.2 %all-to-all-done.5 = bf16[16,256,1024]{2,1,0:T(8,128)(2,1)} async-done(((bf16[16,256,1024]{2,1,0:T(8,128)(2,1)}), bf16[16,256,1024]{2,1,0:T(8,128)(2,1)}, u32[]{:S(2)}, u32[]{:S(2)}) %all-to-all-start.5) | async-done | bytes 8388640 | tf_op jit(solution)/shard_map/all_to_all | solution.py:152
  719.9 15.5 %gather_fusion = bf16[2048,1024]{1,0:T(8,128)(2,1)} fusion(bf16[4096,1024]{1,0:T(8,128)(2,1)} %bitcast.46, s32[2048]{0:T(1024)S(1)} %broadcast_clamp_fusion), kind=kCustom, calls=%fused_computation.1 | custom fusion | bytes 8396800 | tf_op jit(solution)/shard_map/gather | solution.py:155
  735.3 4.8 fusion.26
  740.1 1.0 add_convert_fusion
  (73 shorter events, 12.0 us)
Async XLA Ops:
  7.2 203.3 %copy-start = (bf16[1024,1024]{1,0:T(8,128)(2,1)S(1)}, bf16[1024,1024]{1,0:T(8,128)(2,1)}, u32[]{:S(2)}) copy-start(bf16[1024,1024]{1,0:T(8,128)(2,1)} %param.20) | copy-start | bytes 6291460
  7.2 16.5 %copy-start.4 = (s32[256,8]{0,1:T(8,128)S(1)}, s32[256,8]{0,1:T(8,128)}, u32[]{:S(2)}) copy-start(s32[256,8]{0,1:T(8,128)} %param.22) | copy-start | bytes 24580
  9.3 10.9 %all-to-all-start.1 = ((bf16[2,128,8,128]{3,1,0,2:T(8,128)(2,1)}), bf16[2,128,8,128]{3,1,0,2:T(8,128)(2,1)S(1)}, u32[]{:S(2)}, u32[]{:S(2)}) async-start(bf16[2,128,8,128]{3,1,0,2:T(8,128)(2,1)} %copy.81), calls=%async_computation.1 | async-start | bytes 1048576 | tf_op jit(solution)/shard_map/all_to_all | solution.py:89
  20.1 9.9 %all-to-all-start.2 = ((bf16[2,128,8,128]{1,3,0,2:T(8,128)(2,1)}), bf16[2,128,8,128]{1,3,0,2:T(8,128)(2,1)S(1)}, u32[]{:S(2)}, u32[]{:S(2)}) async-start(bf16[2,128,8,128]{1,3,0,2:T(8,128)(2,1)} %copy.84), calls=%async_computation.2 | async-start | bytes 1048576 | tf_op jit(solution)/shard_map/all_to_all | solution.py:90
  29.0 12.1 %copy-start.10 = (s32[32]{0:T(128)S(1)}, s32[32]{0:T(128)}, u32[]{:S(2)}) copy-start(s32[32]{0:T(128)} %param.18) | copy-start | bytes 388
  29.0 12.2 %copy-start.9 = (s32[2,128]{1,0:T(2,128)S(1)}, s32[2,128]{1,0:T(2,128)}, u32[]{:S(2)}) copy-start(s32[2,128]{1,0:T(2,128)} %param.25) | copy-start | bytes 3076
  29.0 16.0 %copy-start.11 = (s32[32]{0:T(128)S(1)}, s32[32]{0:T(128)}, u32[]{:S(2)}) copy-start(s32[32]{0:T(128)} %param.19) | copy-start | bytes 388
  30.1 50.6 %all-to-all-start = ((bf16[2,1024,8,128]{3,1,0,2:T(8,128)(2,1)}), bf16[2,1024,8,128]{3,1,0,2:T(8,128)(2,1)}, u32[]{:S(2)}, u32[]{:S(2)}) async-start(bf16[2,1024,8,128]{3,1,0,2:T(8,128)(2,1)} %copy.78), calls=%async_computation | async-start | bytes 8388608 | tf_op jit(solution)/shard_map/all_to_all | solution.py:88
  85.3 107.8 %copy-start.8 = (s32[256]{0:T(256)S(1)}, s32[256]{0:T(256)}, u32[]{:S(2)}) copy-start(s32[256]{0:T(256)} %compare_select_fusion.3) | copy-start | bytes 3076
  85.3 107.8 %copy-start.1 = (s32[256]{0:T(256)S(1)}, s32[256]{0:T(256)}, u32[]{:S(2)}) copy-start(s32[256]{0:T(256)} %get-tuple-element.133) | copy-start | bytes 3076
  92.3 2.8 copy-start.2
  92.3 3.5 copy-start.3
  144.4 2.8 copy-start.2
  144.4 3.5 copy-start.3
  189.4 23.1 %copy-start.7 = (f32[1024]{0:T(1024)S(1)}, f32[1024]{0:T(1024)}, u32[]{:S(2)}) copy-start(f32[1024]{0:T(1024)} %param.21) | copy-start | bytes 12292
  189.4 9.0 %all-to-all-start.3 = ((bf16[2,256,4,128]{3,2,0,1:T(4,128)(2,1)}), bf16[2,256,4,128]{3,2,0,1:T(4,128)(2,1)S(1)}, u32[]{:S(2)}, u32[]{:S(2)}) async-start(bf16[2,256,4,128]{3,2,0,1:T(4,128)(2,1)} %get-tuple-element.80), calls=%async_computation.3 | async-start | bytes 1048576 | tf_op jit(solution)/shard_map/all_to_all | solution.py:93
  195.0 18.4 %copy-start.5 = (s32[2048,1]{0,1:T(1,128)S(1)}, s32[2048,1]{0,1:T(1,128)}, u32[]{:S(2)}) copy-start(s32[2048,1]{0,1:T(1,128)} %compare_select_fusion.1) | copy-start | bytes 24580
  198.4 48.0 %all-to-all-start.6 = ((s32[16,1,16]{2,1,0:T(1,128)}), s32[16,1,16]{2,1,0:T(1,128)S(1)}, u32[]{:S(2)}, u32[]{:S(2)}) async-start(s32[16,1,16]{2,1,0:T(1,128)} %all_to_all.84), calls=%async_computation.6 | async-start | bytes 16384 | tf_op jit(solution)/shard_map/all_to_all | solution.py:109
  246.4 188.6 %all-to-all-start.4 = ((bf16[16,256,1024]{2,1,0:T(8,128)(2,1)}), bf16[16,256,1024]{2,1,0:T(8,128)(2,1)}, u32[]{:S(2)}, u32[]{:S(2)}) async-start(bf16[16,256,1024]{2,1,0:T(8,128)(2,1)} %bitcast.189), calls=%async_computation.4 | async-start | bytes 16777216 | tf_op jit(solution)/shard_map/all_to_all | solution.py:139
  435.0 97.4 %all-to-all-start.7 = ((bf16[16,16,4,16,128]{4,3,2,1,0:T(8,128)(2,1)}), bf16[16,16,4,16,128]{4,3,2,1,0:T(8,128)(2,1)}, u32[]{:S(2)}, u32[]{:S(2)}) async-start(bf16[16,16,4,16,128]{4,3,2,1,0:T(8,128)(2,1)} %bitcast.192), calls=%async_computation.7 | async-start | bytes 8388608 | tf_op jit(solution)/shard_map/all_to_all | solution.py:108
  439.9 46.9 %all-gather.2.cloned.1.call-start = ((), (), s32[]{:S(2)}) async-start(), calls=%async_computation.8 | async-start | bytes 4718592 | tf_op jit(solution)/shard_map/all_gather | solution.py:138
  514.2 23.5 %copy-start.6 = (f32[256,8]{0,1:T(8,128)S(1)}, f32[256,8]{0,1:T(8,128)}, u32[]{:S(2)}) copy-start(f32[256,8]{0,1:T(8,128)} %param.23) | copy-start | bytes 24580
  532.4 187.5 %all-to-all-start.5 = ((bf16[16,256,1024]{2,1,0:T(8,128)(2,1)}), bf16[16,256,1024]{2,1,0:T(8,128)(2,1)}, u32[]{:S(2)}, u32[]{:S(2)}) async-start(bf16[16,256,1024]{2,1,0:T(8,128)(2,1)} %convolution_convert_fusion), calls=%async_computation.5 | async-start | bytes 16777216 | tf_op jit(solution)/shard_map/all_to_all | solution.py:152
Sparse Core Ops, SparseCore 0:
  442.3 44.5 all-gather.1
where the time goes:
time: 760 us; the launch traced here: 748 us
  waiting for transfers between devices  417 us (55%)
  local copies, waits for them, and re-layouts  147 us (19%)
  other arithmetic  68.1 us (9%)
  matrix products  58.8 us (8%)
  starting transfers between devices  43.5 us (6%)
  between operations  14.8 us (2%)
    all_to_all x1, waiting for transfers between devices, body(): lax.all_to_all(buffer, 'req', split_axis=0, concat_axis=0, tiled=True)  170 us
    all_to_all x1, waiting for transfers between devices, body(): lax.all_to_all(expert_out.reshape(slot_block.shape), 'req', split_axis=0,...  144 us
    all_gather x1, waiting for transfers between devices, body(): full_weights = lax.all_gather(w_experts, 'kv', axis=3, tiled=True)  46.2 us
    sub x2, other arithmetic, soft_weights(): probability = jnp.where(allowed, jnp.exp(masked - row_max), 0.0)  38.9 us
    scatter x1, local copies, waits for them, and re-layouts, body(): decode_pool = jnp.zeros((slots_dev, group_count, BLOCK, head_pair), jnp.b...  33.5 us
    scatter x1, local copies, waits for them, and re-layouts, body(): buffer = jnp.zeros((experts * capacity, width_model), jnp.bfloat16).at[ta...  33 us
    all_to_all x1, waiting for transfers between devices, body(): lax.all_to_all(cache, 'kv', split_axis=2, concat_axis=1, tiled=True)  28.7 us
    dynamic_slice x10, local copies, waits for them, and re-layouts, body(): lax.map(whole_request, (query_heads, cache_heads, span_heads, lengths))  20.2 us
  transfers between devices with their start and end apart: 9, of which 8 were waited for; matrix products, arithmetic and copies ran while one was open for 19% of the time, Pallas kernels for 0%

commit v1 on v0

--- a/solution.py
+++ b/solution.py
@@ -5,6 +5,13 @@
 from jax.sharding import PartitionSpec as P
 
 BLOCK = 16
+
+
+def stacked_exchange(block, name, split, join):
+    size = lax.axis_size(name)
+    parts = jnp.stack(jnp.split(block, size, axis=split), axis=0)
+    parts = lax.all_to_all(parts, name, split_axis=0, concat_axis=0)
+    return jnp.concatenate(parts, axis=join)
 
 
 def lookup_lengths(req_order, cached_len, count):
@@ -85,7 +92,7 @@
     lengths = lookup_lengths(req_order, cached_len, local_reqs)
     queries_grouped = queries.reshape(local_reqs, local_tokens, kv_heads, group_width)
     cache_heads, span_heads, query_heads = (
-        lax.all_to_all(cache, "kv", split_axis=2, concat_axis=1, tiled=True),
+        stacked_exchange(cache, "kv", 2, 1),
         lax.all_to_all(span_kv, "kv", split_axis=2, concat_axis=1, tiled=True),
         lax.all_to_all(queries_grouped, "kv", split_axis=2, concat_axis=1, tiled=True),
     )

time: 760 us -> 759 us (level)
  transfers between devices with their start and end apart: 9 -> 9, of which waited for: 8 -> 6; matrix products, arithmetic and copies ran while one was open for 19% -> 20% of each run, Pallas kernels for 0% -> 0%
where the time goes in v1:
time: 759 us; the launch traced here: 754 us
  waiting for transfers between devices  413 us (54%)
  local copies, waits for them, and re-layouts  153 us (20%)
  other arithmetic  72.7 us (10%)
  matrix products  58.8 us (8%)
  starting transfers between devices  42.1 us (6%)
  between operations  14.6 us (2%)
    all_to_all x1, waiting for transfers between devices, body(): lax.all_to_all(buffer, 'req', split_axis=0, concat_axis=0, tiled=True)  170 us
    all_to_all x1, waiting for transfers between devices, body(): lax.all_to_all(expert_out.reshape(slot_block.shape), 'req', split_axis=0,...  144 us
    all_gather x1, waiting for transfers between devices, body(): full_weights = lax.all_gather(w_experts, 'kv', axis=3, tiled=True)  46.2 us
    sub x2, other arithmetic, soft_weights(): probability = jnp.where(allowed, jnp.exp(masked - row_max), 0.0)  38.9 us
    scatter x1, local copies, waits for them, and re-layouts, body(): decode_pool = jnp.zeros((slots_dev, group_count, BLOCK, head_pair), jnp.b...  33.5 us
    scatter x1, local copies, waits for them, and re-layouts, body(): buffer = jnp.zeros((experts * capacity, width_model), jnp.bfloat16).at[ta...  33 us
    all_to_all x1, waiting for transfers between devices, stacked_exchange(): parts = lax.all_to_all(parts, name, split_axis=0, concat_axis=0)  30.5 us
    dynamic_slice x10, local copies, waits for them, and re-layouts, body(): lax.map(whole_request, (query_heads, cache_heads, span_heads, lengths))  20.2 us
  transfers between devices with their start and end apart: 9, of which 6 were waited for; matrix products, arithmetic and copies ran while one was open for 20% of the time, Pallas kernels for 0%

profile of v1, /device:TPU:11, one launch (start us, length us, event | category | flops | bytes accessed | tf_op | source)
XLA Modules:
  0.0 754.5 jit_solution(14967789713718527178)
XLA Ops:
  7.2 2.1 copy.67
  9.3 3.5 all-to-all-start.1
  12.8 6.3 fusion.47
  19.1 1.3 copy.69
  20.4 0.8 copy.70
  21.3 3.5 all-to-all-start.2
  24.8 5.1 copy_bitcast_fusion
  30.2 4.6 pad_maximum_fusion
  34.9 6.3 all-to-all-start
  41.2 4.5 reduce-window.6
  47.3 3.2 sort.17
  53.2 1.1 copy.68
  54.3 2.2 all_to_all.59
  56.4 1.0 copy.72
  57.5 30.5 %all-to-all-done = bf16[2,2,1024,4,128]{4,2,3,1,0:T(8,128)(2,1)} async-done(((bf16[2,2,1024,4,128]{4,2,3,1,0:T(8,128)(2,1)}), bf16[2,2,1024,4,128]{4,2,3,1,0:T(8,128)(2,1)}, u32[]{:S(2)}, u32[]{:S(2)}) %all-to-all-start) | async-done | bytes 4194336 | tf_op jit(solution)/shard_map/all_to_all | solution.py:13
  87.9 4.6 copy.66
  92.5 104.1 %while.12 = (s32[]{:T(128)}, bf16[2,256,4,128]{3,2,0,1:T(4,128)(2,1)}, bf16[2,2048,4,128]{3,1,2,0:T(8,128)(2,1)}, bf16[2,256,4,128]{1,3,2,0:T(8,128)(2,1)}, s32[...) while((s32[]{:T(128)}, bf16[2,256,4,128]{3,2,0,1:T(4,128)(2,1)}, ...), condition=%wide.region_4.5_spmd, body=%wide.region_1.4_spmd.sunk | while | flops 1251877888 | bytes 80653984 | solution.py:99
  92.5 3.0 constant_dynamic-slice_fusion.5
  95.6 4.0 copy.102
  99.6 2.8 fusion.65
  103.1 0.7 constant_dynamic-slice_fusion.4
  103.8 1.1 copy.101
  104.9 9.2 %fusion.66 = f32[4,2304,256,2]{2,1,3,0:T(8,128)} fusion(bf16[256,4,2,64]{0,3,2,1:T(8,128)(2,1)S(1)} %bitcast.192, bf16[256,4,64]{0,2,1:T(8,128)(2,1)} %get-tuple-element.181, bf16[2048,4,64]{0,2,1:T(8,128)(2,1)} %get-tuple-element.182), kind=kOutput, calls=%fused_computation.24.clone.1 | convolution fusion | flops 606339072 | bytes 20316160 | tf_op jit(solution)/shard_map/while/body/eval_jaxpr/igsd,pgd->gsip/dot_general | solution.py:31
  114.1 1.2 dynamic_slice.41
  116.0 2.7 fusion.67
  118.7 19.4 %fusion.68 = (f32[4,2,256]{2,1,0:T(2,128)S(1)}, bf16[4,2,256,2304]{2,3,1,0:T(8,128)(2,1)}) fusion(f32[4,2304,256,2]{2,1,3,0:T(8,128)} %fusion.66, pred[256,2304]{0,1:T(8,128)(4,1)} %fusion.67), kind=kOutput, calls=%fused_computation.102.clone.1 | output fusion | flops 37751040 | bytes 28909568 | tf_op jit(solution)/shard_map/while/body/eval_jaxpr/sub | solution.py:40
  138.2 5.5 fusion.69
  143.8 0.8 constant_dynamic-update-slice_fusion.2
  144.6 3.0 constant_dynamic-slice_fusion.5
  147.6 4.0 copy.102
  151.6 2.8 fusion.65
  155.1 0.7 constant_dynamic-slice_fusion.4
  155.9 1.1 copy.101
  157.0 9.2 %fusion.66 = f32[4,2304,256,2]{2,1,3,0:T(8,128)} fusion(bf16[256,4,2,64]{0,3,2,1:T(8,128)(2,1)S(1)} %bitcast.192, bf16[256,4,64]{0,2,1:T(8,128)(2,1)} %get-tuple-element.181, bf16[2048,4,64]{0,2,1:T(8,128)(2,1)} %get-tuple-element.182), kind=kOutput, calls=%fused_computation.24.clone.1 | convolution fusion | flops 606339072 | bytes 20316160 | tf_op jit(solution)/shard_map/while/body/eval_jaxpr/igsd,pgd->gsip/dot_general | solution.py:31
  166.2 1.2 dynamic_slice.41
  168.1 2.7 fusion.67
  170.8 19.4 %fusion.68 = (f32[4,2,256]{2,1,0:T(2,128)S(1)}, bf16[4,2,256,2304]{2,3,1,0:T(8,128)(2,1)}) fusion(f32[4,2304,256,2]{2,1,3,0:T(8,128)} %fusion.66, pred[256,2304]{0,1:T(8,128)(4,1)} %fusion.67), kind=kOutput, calls=%fused_computation.102.clone.1 | output fusion | flops 37751040 | bytes 28909568 | tf_op jit(solution)/shard_map/while/body/eval_jaxpr/sub | solution.py:40
  190.2 5.5 fusion.69
  195.9 0.8 constant_dynamic-update-slice_fusion.2
  196.7 3.6 all-to-all-start.3
  200.3 1.9 gather_fusion.1
  203.7 3.1 all-to-all-done.3
  206.8 8.6 %all-to-all-start.6 = ((s32[16,1,16]{2,1,0:T(1,128)}), s32[16,1,16]{2,1,0:T(1,128)S(1)}, u32[]{:S(2)}, u32[]{:S(2)}) async-start(s32[16,1,16]{2,1,0:T(1,128)} %all_to_all.69), calls=%async_computation.6 | async-start | bytes 16384 | tf_op jit(solution)/shard_map/all_to_all | solution.py:116
  215.6 1.2 reshape.277
  216.7 2.0 multiply_reduce_fusion
  218.7 0.9 multiply_convert_fusion
  219.7 33.0 %scatter_custom_fusion = bf16[4096,1024]{1,0:T(8,128)(2,1)} fusion(s32[2048]{0:T(1024)S(1)} %bitcast.207, bf16[256,1024]{1,0:T(8,128)(2,1)} %multiply_convert_fusion, s32[2048]{0:T(1024)S(1)} %broadcast_clamp_fusion.1, bf16[]{:T(256)} %constant.114.clone.1), kind=kCustom, calls=%fused_computation.50 | custom fusion | bytes 8389120 | tf_op jit(solution)/shard_map/scatter | solution.py:142
  252.7 6.4 all-to-all-start.4
  259.8 2.6 select_bitcast_fusion
  262.4 3.3 copy.81
  265.7 5.2 gather_fusion.2
  270.9 170.4 %all-to-all-done.4 = bf16[16,256,1024]{2,1,0:T(8,128)(2,1)} async-done(((bf16[16,256,1024]{2,1,0:T(8,128)(2,1)}), bf16[16,256,1024]{2,1,0:T(8,128)(2,1)}, u32[]{:S(2)}, u32[]{:S(2)}) %all-to-all-start.4) | async-done | bytes 8388640 | tf_op jit(solution)/shard_map/all_to_all | solution.py:146
  441.3 4.9 all-to-all-start.7
  446.9 46.2 %all-gather.2.cloned.1.call-done = bf16[1,3,1024,512]{3,2,1,0:T(8,128)(2,1)} async-done(((bf16[1,3,1024,256]{3,2,1,0:T(8,128)(2,1)}), bf16[1,3,1024,512]{3,2,1,0:T(8,128)(2,1)}) %all-gather.2.cloned.1.call-update) | async-done | bytes 3145744 | tf_op jit(solution)/shard_map/all_gather | solution.py:145
  493.1 11.4 %fusion.38 = f32[16,256,512]{2,1,0:T(8,128)} fusion(bf16[16,256,1024]{2,1,0:T(8,128)(2,1)} %all-to-all-done.4, bf16[1,3,1024,512]{3,2,1,0:T(8,128)(2,1)} %all-gather.2.cloned.1.call-done), kind=kOutput, calls=%fused_computation.61 | convolution fusion | flops 4294967296 | bytes 17825792 | tf_op jit(solution)/shard_map/sejd,edf->sejf/dot_general | solution.py:149
  504.4 16.0 %convolution_convert_fusion = bf16[16,256,1024]{2,1,0:T(8,128)(2,1)} fusion(f32[16,256,512]{2,1,0:T(8,128)} %fusion.38, bf16[16,256,1024]{2,1,0:T(8,128)(2,1)} %all-to-all-done.4, bf16[1,3,1024,512]{3,2,1,0:T(8,128)(2,1)} %all-gather.2.cloned.1.call-done), kind=kOutput, calls=%fused_computation.47 | convolution fusion | flops 8606711808 | bytes 27262976 | tf_op jit(solution)/shard_map/sejf,edf->sejd/dot_general | solution.py:156
  520.4 18.2 %all-to-all-done.7 = bf16[16,16,4,16,128]{4,3,2,1,0:T(8,128)(2,1)} async-done(((bf16[16,16,4,16,128]{4,3,2,1,0:T(8,128)(2,1)}), bf16[16,16,4,16,128]{4,3,2,1,0:T(8,128)(2,1)}, u32[]{:S(2)}, u32[]{:S(2)}) %all-to-all-start.7) | async-done | bytes 4194336 | tf_op jit(solution)/shard_map/all_to_all | solution.py:115
  538.6 5.3 all-to-all-start.5
  545.4 3.1 broadcast_in_dim.106
  548.4 33.5 %scatter_fusion = bf16[256,4,16,128]{3,2,1,0:T(8,128)(2,1)} fusion(bf16[256,4,16,128]{3,2,1,0:T(8,128)(2,1)} %broadcast_in_dim.106, s32[256]{0:T(256)S(1)} %bitcast.211, bf16[256,4,16,128]{3,2,1,0:T(8,128)(2,1)} %bitcast.55), kind=kCustom, calls=%fused_computation.5 | custom fusion | bytes 12583936 | tf_op jit(solution)/shard_map/scatter | solution.py:123
  581.9 144.2 %all-to-all-done.5 = bf16[16,256,1024]{2,1,0:T(8,128)(2,1)} async-done(((bf16[16,256,1024]{2,1,0:T(8,128)(2,1)}), bf16[16,256,1024]{2,1,0:T(8,128)(2,1)}, u32[]{:S(2)}, u32[]{:S(2)}) %all-to-all-start.5) | async-done | bytes 8388640 | tf_op jit(solution)/shard_map/all_to_all | solution.py:159
  726.1 15.5 %gather_fusion = bf16[2048,1024]{1,0:T(8,128)(2,1)} fusion(bf16[4096,1024]{1,0:T(8,128)(2,1)} %bitcast.46, s32[2048]{0:T(1024)S(1)} %broadcast_clamp_fusion), kind=kCustom, calls=%fused_computation.1 | custom fusion | bytes 8396800 | tf_op jit(solution)/shard_map/gather | solution.py:162
  741.6 4.8 fusion.26
  746.4 1.0 add_convert_fusion
  (75 shorter events, 12.0 us)
Async XLA Ops:
  7.2 209.5 %copy-start = (bf16[1024,1024]{1,0:T(8,128)(2,1)S(1)}, bf16[1024,1024]{1,0:T(8,128)(2,1)}, u32[]{:S(2)}) copy-start(bf16[1024,1024]{1,0:T(8,128)(2,1)} %param.20) | copy-start | bytes 6291460
  9.3 12.0 %all-to-all-start.1 = ((bf16[2,128,8,128]{3,1,0,2:T(8,128)(2,1)}), bf16[2,128,8,128]{3,1,0,2:T(8,128)(2,1)S(1)}, u32[]{:S(2)}, u32[]{:S(2)}) async-start(bf16[2,128,8,128]{3,1,0,2:T(8,128)(2,1)} %copy.67), calls=%async_computation.1 | async-start | bytes 1048576 | tf_op jit(solution)/shard_map/all_to_all | solution.py:96
  21.3 13.6 %all-to-all-start.2 = ((bf16[2,128,8,128]{1,3,0,2:T(8,128)(2,1)}), bf16[2,128,8,128]{1,3,0,2:T(8,128)(2,1)S(1)}, u32[]{:S(2)}, u32[]{:S(2)}) async-start(bf16[2,128,8,128]{1,3,0,2:T(8,128)(2,1)} %copy.70), calls=%async_computation.2 | async-start | bytes 1048576 | tf_op jit(solution)/shard_map/all_to_all | solution.py:97
  24.8 5.1 copy-start.4
  34.9 11.7 %copy-start.10 = (s32[32]{0:T(128)S(1)}, s32[32]{0:T(128)}, u32[]{:S(2)}) copy-start(s32[32]{0:T(128)} %param.18) | copy-start | bytes 388
  34.9 11.8 %copy-start.9 = (s32[2,128]{1,0:T(2,128)S(1)}, s32[2,128]{1,0:T(2,128)}, u32[]{:S(2)}) copy-start(s32[2,128]{1,0:T(2,128)} %param.25) | copy-start | bytes 3076
  34.9 15.6 %copy-start.11 = (s32[32]{0:T(128)S(1)}, s32[32]{0:T(128)}, u32[]{:S(2)}) copy-start(s32[32]{0:T(128)} %param.19) | copy-start | bytes 388
  34.9 53.1 %all-to-all-start = ((bf16[2,2,1024,4,128]{4,2,3,1,0:T(8,128)(2,1)}), bf16[2,2,1024,4,128]{4,2,3,1,0:T(8,128)(2,1)}, u32[]{:S(2)}, u32[]{:S(2)}) async-start(bf16[2,2,1024,4,128]{4,2,3,1,0:T(8,128)(2,1)} %pad_maximum_fusion), calls=%async_computation | async-start | bytes 8388608 | tf_op jit(solution)/shard_map/all_to_all | solution.py:13
  92.5 107.8 %copy-start.8 = (s32[256]{0:T(256)S(1)}, s32[256]{0:T(256)}, u32[]{:S(2)}) copy-start(s32[256]{0:T(256)} %compare_select_fusion.3) | copy-start | bytes 3076
  92.5 107.8 %copy-start.1 = (s32[256]{0:T(256)S(1)}, s32[256]{0:T(256)}, u32[]{:S(2)}) copy-start(s32[256]{0:T(256)} %get-tuple-element.129) | copy-start | bytes 3076
  99.6 2.8 copy-start.2
  99.6 3.5 copy-start.3
  151.6 2.8 copy-start.2
  151.6 3.5 copy-start.3
  196.7 22.1 %copy-start.7 = (f32[1024]{0:T(1024)S(1)}, f32[1024]{0:T(1024)}, u32[]{:S(2)}) copy-start(f32[1024]{0:T(1024)} %param.21) | copy-start | bytes 12292
  196.7 10.1 %all-to-all-start.3 = ((bf16[2,256,4,128]{3,2,0,1:T(4,128)(2,1)}), bf16[2,256,4,128]{3,2,0,1:T(4,128)(2,1)S(1)}, u32[]{:S(2)}, u32[]{:S(2)}) async-start(bf16[2,256,4,128]{3,2,0,1:T(4,128)(2,1)} %get-tuple-element.80), calls=%async_computation.3 | async-start | bytes 1048576 | tf_op jit(solution)/shard_map/all_to_all | solution.py:100
  202.3 17.4 %copy-start.5 = (s32[2048,1]{0,1:T(1,128)S(1)}, s32[2048,1]{0,1:T(1,128)}, u32[]{:S(2)}) copy-start(s32[2048,1]{0,1:T(1,128)} %compare_select_fusion.1) | copy-start | bytes 24580
  206.8 45.9 %all-to-all-start.6 = ((s32[16,1,16]{2,1,0:T(1,128)}), s32[16,1,16]{2,1,0:T(1,128)S(1)}, u32[]{:S(2)}, u32[]{:S(2)}) async-start(s32[16,1,16]{2,1,0:T(1,128)} %all_to_all.69), calls=%async_computation.6 | async-start | bytes 16384 | tf_op jit(solution)/shard_map/all_to_all | solution.py:116
  252.7 188.6 %all-to-all-start.4 = ((bf16[16,256,1024]{2,1,0:T(8,128)(2,1)}), bf16[16,256,1024]{2,1,0:T(8,128)(2,1)}, u32[]{:S(2)}, u32[]{:S(2)}) async-start(bf16[16,256,1024]{2,1,0:T(8,128)(2,1)} %bitcast.191), calls=%async_computation.4 | async-start | bytes 16777216 | tf_op jit(solution)/shard_map/all_to_all | solution.py:146
  441.3 97.4 %all-to-all-start.7 = ((bf16[16,16,4,16,128]{4,3,2,1,0:T(8,128)(2,1)}), bf16[16,16,4,16,128]{4,3,2,1,0:T(8,128)(2,1)}, u32[]{:S(2)}, u32[]{:S(2)}) async-start(bf16[16,16,4,16,128]{4,3,2,1,0:T(8,128)(2,1)} %bitcast.194), calls=%async_computation.7 | async-start | bytes 8388608 | tf_op jit(solution)/shard_map/all_to_all | solution.py:115
  446.1 46.9 %all-gather.2.cloned.1.call-start = ((), (), s32[]{:S(2)}) async-start(), calls=%async_computation.8 | async-start | bytes 4718592 | tf_op jit(solution)/shard_map/all_gather | solution.py:145
  520.4 23.5 %copy-start.6 = (f32[256,8]{0,1:T(8,128)S(1)}, f32[256,8]{0,1:T(8,128)}, u32[]{:S(2)}) copy-start(f32[256,8]{0,1:T(8,128)} %param.23) | copy-start | bytes 24580
  538.6 187.5 %all-to-all-start.5 = ((bf16[16,256,1024]{2,1,0:T(8,128)(2,1)}), bf16[16,256,1024]{2,1,0:T(8,128)(2,1)}, u32[]{:S(2)}, u32[]{:S(2)}) async-start(bf16[16,256,1024]{2,1,0:T(8,128)(2,1)} %convolution_convert_fusion), calls=%async_computation.5 | async-start | bytes 16777216 | tf_op jit(solution)/shard_map/all_to_all | solution.py:159
Sparse Core Ops, SparseCore 0:
  448.5 44.5 all-gather.1
